TPU v7x, 128 devices: a whole 4x4x4 slice. The times are simulated.
128 devices in a mesh: blk: 16 (over x, y_hi, core), req: 8 (over y_lo, z).
Axes of the slice: x: 4, y: 4 (y_hi: 2, y_lo: 2; y = y_hi * 2 + y_lo), z: 4, core: 2. Of those that a mesh axis runs over, the one named last changes fastest.
Arguments:
- long_q: bfloat16 [16384, 2048], P('blk', 'req'), may hold values from -6 to 6
- long_k: bfloat16 [16384, 2048], P('blk', 'req'), may hold values from -6 to 6
- long_v: bfloat16 [16384, 2048], P('blk', 'req'), may hold values from -6 to 6
- short_q: bfloat16 [8192, 2048], P('blk', 'req'), may hold values from -6 to 6
- short_k: bfloat16 [8192, 2048], P('blk', 'req'), may hold values from -6 to 6
- short_v: bfloat16 [8192, 2048], P('blk', 'req'), may hold values from -6 to 6
- short_seg: int32 [16, 512], P('blk'), may hold values from 0 to 15, never falling along the last dimension, each value on 1 to 96 neighbouring positions
- pool_kv: bfloat16 [1024, 2, 16, 2048], P('blk', None, None, 'req'), may hold values from -6 to 6
- page_table: int32 [16, 16, 4], replicated, may hold values from 0 to 1023, as said below
- w_out: bfloat16 [2048, 2048], replicated, may hold values from -0.125 to 0.125
Outputs:
- long_out: bfloat16 [16384, 2048], P(('blk', 'req'))
- short_out: bfloat16 [8192, 2048], P(('blk', 'req'))
Inputs may be any that keep to these rules, and one draw needn't show every extreme that they name: `short_seg`: along each pack the request numbers never fall, and each of the 16 requests has 1 to 96 tokens, one of them exactly 96. `page_table`: entry [b, s, j] is o * 64 + i for page i of the pool rows held by index o of blk; for every pack b and every o exactly 4 of the 64 entries of b name pages of o.
All inputs are finite; a program needn't handle non-finite values.
Results may differ from a plain program's by a relative error of at most 0.015.
Values may be sent and summed in bfloat16 or wider, within the bound.
No kernel may reach another device: no remote copies, remote signals or barrier semaphores. Data moves between devices by JAX's collectives and lax.ppermute only.
A program may use at most 128 MiB of HBM per device.

v0:
```python
import math
import jax
import jax.numpy as jnp
from jax import lax
from jax.sharding import PartitionSpec as P

HD = 128
PPS = 4
very_negative = -1e30


def fold_block(state_now, query_heads, query_pos, key_block, value_block, block_first):
    acc_sum, run_max, run_total = state_now
    heads_dev = query_heads.shape[1]
    key_heads = key_block.reshape(key_block.shape[0], heads_dev, HD)
    value_heads = value_block.reshape(value_block.shape[0], heads_dev, HD)
    scores = jnp.einsum(
        "qhd,khd->hqk", query_heads, key_heads, preferred_element_type=jnp.float32
    ) * HD ** (-0.5)
    key_pos = block_first + jnp.arange(key_block.shape[0], dtype=jnp.int32)
    allowed = (key_pos[None, :] <= query_pos[:, None])[None]
    scores = jnp.where(allowed, scores, very_negative)
    new_max = jnp.maximum(run_max, jnp.max(scores, axis=-1))
    weights = jnp.where(allowed, jnp.exp(scores - new_max[..., None]), 0.0)
    factor = jnp.exp(run_max - new_max)
    run_total = run_total * factor + jnp.sum(weights, axis=-1)
    acc_sum = acc_sum * factor[..., None] + jnp.einsum(
        "hqk,khd->hqd",
        weights.astype(jnp.bfloat16),
        value_heads,
        preferred_element_type=jnp.float32,
    )
    return (acc_sum, new_max, run_total)


def prompt_attention(queries, query_pos, long_k, long_v):
    row_count, width = queries.shape
    heads_dev = width // HD
    query_heads = queries.reshape(row_count, heads_dev, HD)
    last_pos = jnp.max(query_pos)
    init = (
        jnp.zeros((heads_dev, row_count, HD), jnp.float32),
        jnp.full((heads_dev, row_count), very_negative, jnp.float32),
        jnp.zeros((heads_dev, row_count), jnp.float32),
    )
    key_piece = lax.all_gather(long_k, "blk", axis=0, tiled=True)
    value_piece = lax.all_gather(long_v, "blk", axis=0, tiled=True)
    piece_rows = key_piece.shape[0]
    step_rows = math.gcd(piece_rows, 1024)

    def one_step(block_num, state_in):
        block_start = block_num * step_rows
        key_block = lax.dynamic_slice_in_dim(key_piece, block_start, step_rows, 0)
        value_block = lax.dynamic_slice_in_dim(value_piece, block_start, step_rows, 0)

        def compute_block(state_live):
            return fold_block(
                state_live, query_heads, query_pos, key_block, value_block, block_start
            )

        def keep_state(state_skip):
            return state_skip

        return lax.cond(block_start <= last_pos, compute_block, keep_state, state_in)

    acc_sum, run_max, run_total = lax.fori_loop(0, piece_rows // step_rows, one_step, init)
    merged = acc_sum / run_total[..., None]
    return merged.transpose(1, 0, 2).reshape(row_count, width).astype(jnp.bfloat16)


def pack_attention(
    short_q, short_k, short_v, short_seg, pool_kv, page_table, block_index, block_count
):
    pack_rows, width = short_q.shape
    heads_dev = width // HD
    pool_pages = pool_kv.shape[0]
    page_len = pool_kv.shape[2]
    page_rows = page_table.reshape(block_count, -1)
    entries = page_rows.shape[1]
    capacity = entries // block_count
    owners = page_rows // pool_pages
    places = page_rows % pool_pages
    wanted = owners == block_index
    ranks = jnp.cumsum(wanted.astype(jnp.int32), axis=1) - 1
    picked = wanted[:, :, None] & (
        ranks[:, :, None] == jnp.arange(capacity, dtype=jnp.int32)[None, None, :]
    )
    send_places = jnp.sum(jnp.where(picked, places[:, :, None], 0), axis=1)
    outgoing = pool_kv[send_places.reshape(-1)].reshape(block_count, capacity, 2, page_len, width)
    arrived = lax.all_to_all(outgoing, "blk", split_axis=0, concat_axis=0, tiled=True)
    my_owners = lax.dynamic_index_in_dim(owners, block_index, 0, keepdims=False)
    order = jnp.arange(entries, dtype=jnp.int32)
    before = (my_owners[None, :] == my_owners[:, None]) & (order[None, :] < order[:, None])
    slots = my_owners * capacity + jnp.sum(before.astype(jnp.int32), axis=1)
    fetched = arrived.reshape(block_count * capacity, 2, page_len, width)[slots]
    cache_len = entries * page_len
    key_rows = jnp.concatenate([fetched[:, 0].reshape(cache_len, width), short_k], 0)
    value_rows = jnp.concatenate([fetched[:, 1].reshape(cache_len, width), short_v], 0)
    segment = short_seg[0]
    positions = jnp.arange(pack_rows, dtype=jnp.int32)
    key_seg = jnp.concatenate([jnp.arange(cache_len, dtype=jnp.int32) // (PPS * page_len), segment])
    key_pos = jnp.concatenate([jnp.full((cache_len,), -1, jnp.int32), positions])
    allowed = ((key_seg[None, :] == segment[:, None]) & (key_pos[None, :] <= positions[:, None]))[
        None
    ]
    query_heads = short_q.reshape(pack_rows, heads_dev, HD)
    key_heads = key_rows.reshape(cache_len + pack_rows, heads_dev, HD)
    value_heads = value_rows.reshape(cache_len + pack_rows, heads_dev, HD)
    scores = jnp.einsum(
        "qhd,khd->hqk", query_heads, key_heads, preferred_element_type=jnp.float32
    ) * HD ** (-0.5)
    scores = jnp.where(allowed, scores, very_negative)
    row_max = jnp.max(scores, axis=-1)
    weights = jnp.where(allowed, jnp.exp(scores - row_max[..., None]), 0.0)
    total = jnp.sum(weights, axis=-1)
    numer = jnp.einsum(
        "hqk,khd->hqd",
        weights.astype(jnp.bfloat16),
        value_heads,
        preferred_element_type=jnp.float32,
    )
    merged = numer / total[..., None]
    return merged.transpose(1, 0, 2).reshape(pack_rows, width).astype(jnp.bfloat16)


def per_device(
    long_q, long_k, long_v, short_q, short_k, short_v, short_seg, pool_kv, page_table, w_out
):
    block_count = lax.axis_size("blk")
    block_index = lax.axis_index("blk")
    group_index = lax.axis_index("req")
    row_count, width = long_q.shape
    query_pos = block_index * row_count + jnp.arange(row_count, dtype=jnp.int32)
    long_attn = prompt_attention(long_q, query_pos, long_k, long_v)
    short_attn = pack_attention(
        short_q, short_k, short_v, short_seg, pool_kv, page_table, block_index, block_count
    )
    w_rows = lax.dynamic_slice_in_dim(w_out, group_index * width, width, 0)
    long_out = lax.psum_scatter(
        jnp.dot(long_attn, w_rows, preferred_element_type=jnp.float32).astype(jnp.bfloat16),
        "req",
        scatter_dimension=0,
        tiled=True,
    )
    short_out = lax.psum_scatter(
        jnp.dot(short_attn, w_rows, preferred_element_type=jnp.float32).astype(jnp.bfloat16),
        "req",
        scatter_dimension=0,
        tiled=True,
    )
    return (long_out, short_out)


def solution(mesh):
    placed = (
        P("blk", "req"),
        P("blk", "req"),
        P("blk", "req"),
        P("blk", "req"),
        P("blk", "req"),
        P("blk", "req"),
        P("blk", None),
        P("blk", None, None, "req"),
        P(),
        P(),
    )
    return jax.shard_map(
        per_device,
        mesh=mesh,
        in_specs=placed,
        out_specs=(P(("blk", "req"), None), P(("blk", "req"), None)),
        check_vma=False,
    )
```

profile of v0, /device:TPU:1, one launch (start us, length us, event | category | flops | bytes accessed | tf_op | source)
XLA Modules:
  0.0 403.9 jit_solution(17348322285215755611)
XLA Ops:
  8.1 2.1 copy.40
  10.3 2.1 copy.42
  12.4 0.8 copy.45
  13.3 0.2 reduce_window_sum.11
  13.6 0.1 select_reduce_fusion
  13.7 0.1 copy.50
  13.8 0.1 reshape.279
  13.9 1.6 gather_fusion
  15.5 8.4 %all-to-all-start = ((bf16[16,4,2,16,256]{4,3,2,1,0:T(8,128)(2,1)}), bf16[16,4,2,16,256]{4,3,2,1,0:T(8,128)(2,1)S(1)}, u32[]{:S(2)}, u32[]{:S(2)}) async-start(bf16[16,4,2,16,256]{4,3,2,1,0:T(8,128)(2,1)} %bitcast.9), calls=%async_computation.1 | async-start | bytes 2097152 | tf_op jit(solution)/shard_map/all_to_all | solution.py:90
  24.0 0.1 copy.51
  24.2 0.8 copy.53
  25.0 0.1 copy.55
  25.2 0.2 convert_reduce_fusion
  25.4 1.9 fusion.20
  27.3 17.5 %all-to-all-done = bf16[16,4,2,16,256]{4,3,2,1,0:T(8,128)(2,1)S(1)} async-done(((bf16[16,4,2,16,256]{4,3,2,1,0:T(8,128)(2,1)}), bf16[16,4,2,16,256]{4,3,2,1,0:T(8,128)(2,1)S(1)}, u32[]{:S(2)}, u32[]{:S(2)}) %all-to-all-start) | async-done | bytes 1048608 | tf_op jit(solution)/shard_map/all_to_all | solution.py:90
  44.8 0.6 gather_fusion.1
  45.4 0.9 fusion.64
  46.3 1.2 concatenate.21
  47.5 0.1 copy.52
  47.5 0.1 concatenate.24
  47.7 0.4 copy.56
  48.1 6.6 %fusion.65 = (f32[2,512]{1,0:T(2,128)S(1)}, bf16[2,512,1536]{1,2,0:T(8,128)(2,1)}) fusion(pred[512,1536]{0,1:T(8,128)(4,1)} %fusion.20, bf16[512,2,128]{2,0,1:T(8,128)(2,1)} %copy.53, bf16[1024,2,128]{2,0,1:T(8,128)(2,1)S(1)} %copy.52, bf16[512,256]{1,0:T(8,128)(2,1)} %param.17), kind=kOutput, calls=%fused_computation.93 | convolution fusion | flops 413664768 | bytes 4984832 | tf_op jit(solution)/shard_map/sub | solution.py:114
  54.7 2.5 fusion.28
  57.2 3.3 convolution_convert_fusion.1
  60.6 0.2 reduce-scatter.3.cloned.1.call-start
  60.8 0.6 add_reduce_fusion
  61.4 0.2 copy.41
  61.7 0.3 copy.43
  61.9 35.7 %all-gather.3.cloned.1.call-done = bf16[16384,256]{0,1:T(8,128)(2,1)} async-done(((bf16[1024,256]{0,1:T(8,128)(2,1)}), bf16[16384,256]{0,1:T(8,128)(2,1)}) %all-gather.3.cloned.1.call-update) | async-done | bytes 8388624 | tf_op jit(solution)/shard_map/all_gather | solution.py:46
  97.6 73.6 %all-gather.5.cloned.1.call-done = bf16[16384,256]{0,1:T(8,128)(2,1)} async-done(((bf16[1024,256]{0,1:T(8,128)(2,1)}), bf16[16384,256]{0,1:T(8,128)(2,1)}) %all-gather.5.cloned.1.call-update) | async-done | bytes 8388624 | tf_op jit(solution)/shard_map/all_gather | solution.py:47
  171.3 0.1 broadcast_in_dim.90
  171.4 30.6 %while.18 = (s32[]{:T(128)}, f32[2,1024,128]{2,1,0:T(8,128)S(1)}, f32[2,1024]{1,0:T(2,128)S(1)}, f32[2,1024]{1,0:T(2,128)S(1)}, s32[]{:T(128)}, /*index=5*/bf16[...) while((s32[]{:T(128)}, f32[2,1024,128]{2,1,0:T(8,128)S(1)}, ...), condition=%wide.region_6.7_spmd.clone, body=%wide.region_1.6_spmd.clone.sunk | while | flops 1102583808 | bytes 35283264 | solution.py:66
  172.0 10.0 %conditional.3 = ((f32[2,1024,128]{2,1,0:T(8,128)S(1)}, f32[2,1024]{1,0:T(2,128)S(1)}, f32[2,1024]{1,0:T(2,128)S(1)})) conditional(s32[]{:T(128)} %convert_element_type.77, (f32[2,1024,128]{2,1,0:T(8,128)S(1)}, f32[2,1024]{1,0:T(2,128)S(1)}, f32[2,1024]{1,0:T(2,128)S(1)}) %tuple.66, (s32[]{:T(128)}, s32[]{:T(128)}, bf16[16384,256]{0,1:T(8,128)(2,1)}, ...), branch_computations={%region_2.0_spmd, %region_3.5_spmd} | conditional | flops 1102583808 | bytes 35278928 | solution.py:64
  172.0 1.3 constant_dynamic-slice_fusion
  173.3 0.7 broadcast_compare_fusion
  174.0 2.0 fusion.2
  176.0 2.3 fusion.3
  178.3 3.7 fusion.8
  182.7 10.0 %conditional.3 = ((f32[2,1024,128]{2,1,0:T(8,128)S(1)}, f32[2,1024]{1,0:T(2,128)S(1)}, f32[2,1024]{1,0:T(2,128)S(1)})) conditional(s32[]{:T(128)} %convert_element_type.77, (f32[2,1024,128]{2,1,0:T(8,128)S(1)}, f32[2,1024]{1,0:T(2,128)S(1)}, f32[2,1024]{1,0:T(2,128)S(1)}) %tuple.66, (s32[]{:T(128)}, s32[]{:T(128)}, bf16[16384,256]{0,1:T(8,128)(2,1)}, ...), branch_computations={%region_2.0_spmd, %region_3.5_spmd} | conditional | flops 1102583808 | bytes 35278928 | solution.py:64
  182.7 1.3 constant_dynamic-slice_fusion
  184.0 0.7 broadcast_compare_fusion
  184.6 2.0 fusion.2
  186.6 2.3 fusion.3
  188.9 3.7 fusion.8
  202.0 0.3 copy.44
  202.4 0.1 divide_convert_fusion
  202.5 4.5 %convolution_convert_fusion = bf16[1024,2048]{1,0:T(8,128)(2,1)} fusion(bf16[1024,256]{0,1:T(8,128)(2,1)S(1)} %bitcast.78, bf16[2048,2048]{1,0:T(8,128)(2,1)} %param.23, s32[]{:T(128)S(6)} %select_n.90), kind=kOutput, calls=%fused_computation.25 | convolution fusion | flops 1075838976 | bytes 5767172 | tf_op jit(solution)/shard_map/dot_general | solution.py:140
  207.0 189.5 %reduce-scatter.3.cloned.1.call-done = bf16[128,2048]{1,0:T(8,128)(2,1)} async-done(((bf16[1024,2048]{1,0:T(8,128)(2,1)}), bf16[128,2048]{1,0:T(8,128)(2,1)}) %reduce-scatter.3.cloned.1.call-update) | async-done | bytes 524304 | tf_op jit(solution)/shard_map/reduce_scatter | solution.py:139
  (71 shorter events, 0.8 us)
Async XLA Ops:
  8.0 5.9 %copy-start = (bf16[64,2,16,256]{3,2,1,0:T(8,128)(2,1)S(1)}, bf16[64,2,16,256]{3,2,1,0:T(8,128)(2,1)}, u32[]{:S(2)}) copy-start(bf16[64,2,16,256]{3,2,1,0:T(8,128)(2,1)} %param.21) | copy-start | bytes 3145732
  8.0 17.4 %copy-start.4 = (s32[1536]{0:T(1024)S(1)}, s32[1536]{0:T(1024)}, u32[]{:S(2)}) copy-start(s32[1536]{0:T(1024)} %constant.138.clone.1) | copy-start | bytes 18436
  8.0 16.0 %copy-start.2 = (bf16[512,256]{1,0:T(8,128)(2,1)S(1)}, bf16[512,256]{1,0:T(8,128)(2,1)}, u32[]{:S(2)}) copy-start(bf16[512,256]{1,0:T(8,128)(2,1)} %param.18) | copy-start | bytes 786436
  8.0 17.0 %copy-start.3 = (bf16[512,256]{1,0:T(8,128)(2,1)S(1)}, bf16[512,256]{1,0:T(8,128)(2,1)}, u32[]{:S(2)}) copy-start(bf16[512,256]{1,0:T(8,128)(2,1)} %param.19) | copy-start | bytes 786436
  8.0 17.4 %copy-start.5 = (s32[1,512]{1,0:T(1,128)S(1)}, s32[1,512]{1,0:T(1,128)}, u32[]{:S(2)}) copy-start(s32[1,512]{1,0:T(1,128)} %param.20) | copy-start | bytes 6148
  8.1 89.6 %all-gather.3.cloned.1.call-start = ((), (), s32[]{:S(2)}) async-start(), calls=%async_computation.3 | async-start | bytes 8912896 | tf_op jit(solution)/shard_map/all_gather | solution.py:46
  10.3 161.0 %all-gather.5.cloned.1.call-start = ((), (), s32[]{:S(2)}) async-start(), calls=%async_computation.4 | async-start | bytes 8912896 | tf_op jit(solution)/shard_map/all_gather | solution.py:47
  15.5 29.3 %all-to-all-start = ((bf16[16,4,2,16,256]{4,3,2,1,0:T(8,128)(2,1)}), bf16[16,4,2,16,256]{4,3,2,1,0:T(8,128)(2,1)S(1)}, u32[]{:S(2)}, u32[]{:S(2)}) async-start(bf16[16,4,2,16,256]{4,3,2,1,0:T(8,128)(2,1)} %bitcast.9), calls=%async_computation.1 | async-start | bytes 2097152 | tf_op jit(solution)/shard_map/all_to_all | solution.py:90
  24.0 183.0 %reduce-scatter.5.cloned.1.call-start = ((), (), s32[]{:S(2)}) async-start(), calls=%async_computation.6 | async-start | bytes 2359296 | tf_op jit(solution)/shard_map/reduce_scatter | solution.py:145
  54.7 6.8 %copy-start.1 = (bf16[1024,256]{1,0:T(8,128)(2,1)S(1)}, bf16[1024,256]{1,0:T(8,128)(2,1)}, u32[]{:S(2)}) copy-start(bf16[1024,256]{1,0:T(8,128)(2,1)} %param.14) | copy-start | bytes 1572868
  60.6 335.9 %reduce-scatter.3.cloned.1.call-start = ((), (), s32[]{:S(2)}) async-start(), calls=%async_computation.5 | async-start | bytes 4718592 | tf_op jit(solution)/shard_map/reduce_scatter | solution.py:139
Sparse Core Ops, SparseCore 0:
  11.9 85.6 all-gather.2
  100.1 71.1 all-gather.4
Sparse Core Ops, SparseCore 1:
  60.7 49.7 reduce-scatter.4
  207.1 189.4 reduce-scatter.2
where the time goes:
time: 405 us; the launch traced here: 404 us
  waiting for transfers between devices  316 us (78%)
  matrix products  28.3 us (7%)
  between operations  15.8 us (4%)
  local copies, waits for them, and re-layouts  14.8 us (4%)
  loops' own time  10.8 us (3%)
  other arithmetic  9.14 us (2%)
  starting transfers between devices  8.79 us (2%)
    reduce_scatter x1, waiting for transfers between devices, per_device(): lax.psum_scatter(jnp.dot(long_attn, w_rows, preferred_element_type=jnp.fl...  189 us
    all_gather x1, waiting for transfers between devices, prompt_attention(): value_piece = lax.all_gather(long_v, 'blk', axis=0, tiled=True)  73.6 us
    all_gather x1, waiting for transfers between devices, prompt_attention(): key_piece = lax.all_gather(long_k, 'blk', axis=0, tiled=True)  35.7 us
    all_to_all x1, waiting for transfers between devices, pack_attention(): lax.all_to_all(outgoing, 'blk', split_axis=0, concat_axis=0, tiled=True)  17.5 us
    another operation x1, loops' own time, prompt_attention(): lax.fori_loop(0, piece_rows // step_rows, one_step, init)  10.4 us
    all_to_all x1, starting transfers between devices, pack_attention(): lax.all_to_all(outgoing, 'blk', split_axis=0, concat_axis=0, tiled=True)  8.45 us
  transfers between devices with their start and end apart: 5, of which 4 were waited for; matrix products, arithmetic and copies ran while one was open for 12% of the time, Pallas kernels for 0%

commit v1 on v0

--- a/solution.py
+++ b/solution.py
@@ -7,6 +7,11 @@
 HD = 128
 PPS = 4
 very_negative = -1e30
+
+
+def swapped_in(x, name, along):
+    sent = jnp.stack([x] * lax.axis_size(name))
+    return jnp.concatenate(lax.all_to_all(sent, name, 0, 0), axis=along)
 
 
 def fold_block(state_now, query_heads, query_pos, key_block, value_block, block_first):
@@ -43,7 +48,7 @@
         jnp.full((heads_dev, row_count), very_negative, jnp.float32),
         jnp.zeros((heads_dev, row_count), jnp.float32),
     )
-    key_piece = lax.all_gather(long_k, "blk", axis=0, tiled=True)
+    key_piece = swapped_in(long_k, "blk", 0)
     value_piece = lax.all_gather(long_v, "blk", axis=0, tiled=True)
     piece_rows = key_piece.shape[0]
     step_rows = math.gcd(piece_rows, 1024)

time: 405 us -> 432 us (1.067)
  local copies, waits for them, and re-layouts: 14.8 us -> 40.1 us
  starting transfers between devices: 8.79 us -> 14.9 us
  waiting for transfers between devices: 316 us -> 311 us
    all_to_all x0 -> x1, waiting for transfers between devices: none -> 121 us  [swapped_in(): return jnp.concatenate(lax.all_to_all(sent, name, 0, 0), axis=along)]
    all_gather x1, waiting for transfers between devices: 73.6 us -> 0.01 us  [prompt_attention(): value_piece = lax.all_gather(long_v, 'blk', axis=0, tiled=True)]
    all_gather x1 -> x0, waiting for transfers between devices: 35.7 us -> none  [prompt_attention(): key_piece = lax.all_gather(long_k, 'blk', axis=0, tiled=True)]
    reduce_scatter x1, waiting for transfers between devices: 189 us -> 171 us  [per_device(): lax.psum_scatter(jnp.dot(long_attn, w_rows, preferred_element_type=jnp.fl...]
    all_to_all x0 -> x1, local copies, waits for them, and re-layouts: none -> 12.3 us  [swapped_in(): return jnp.concatenate(lax.all_to_all(sent, name, 0, 0), axis=along)]
    unnamed x19 -> x22, local copies, waits for them, and re-layouts: 5.82 us -> 17 us
    all_to_all x0 -> x1, starting transfers between devices: none -> 6.18 us  [swapped_in(): return jnp.concatenate(lax.all_to_all(sent, name, 0, 0), axis=along)]
  transfers between devices with their start and end apart: 5 -> 5, of which waited for: 4 -> 3; matrix products, arithmetic and copies ran while one was open for 12% -> 17% of each run, Pallas kernels for 0% -> 0%
where the time goes in v1:
time: 432 us; the launch traced here: 430 us
  waiting for transfers between devices  311 us (72%)
  local copies, waits for them, and re-layouts  40.1 us (9%)
  matrix products  27.9 us (6%)
  between operations  15.8 us (4%)
  starting transfers between devices  14.9 us (3%)
  loops' own time  11.7 us (3%)
  other arithmetic  8.48 us (2%)
    reduce_scatter x1, waiting for transfers between devices, per_device(): lax.psum_scatter(jnp.dot(long_attn, w_rows, preferred_element_type=jnp.fl...  171 us
    all_to_all x1, waiting for transfers between devices, swapped_in(): return jnp.concatenate(lax.all_to_all(sent, name, 0, 0), axis=along)  121 us
    all_to_all x1, waiting for transfers between devices, pack_attention(): lax.all_to_all(outgoing, 'blk', split_axis=0, concat_axis=0, tiled=True)  19.3 us
    unnamed x22, local copies, waits for them, and re-layouts  17 us
    all_to_all x1, local copies, waits for them, and re-layouts, swapped_in(): return jnp.concatenate(lax.all_to_all(sent, name, 0, 0), axis=along)  12.3 us
    another operation x1, loops' own time, prompt_attention(): lax.fori_loop(0, piece_rows // step_rows, one_step, init)  11.3 us
  transfers between devices with their start and end apart: 5, of which 3 were waited for; matrix products, arithmetic and copies ran while one was open for 17% of the time, Pallas kernels for 0%

profile of v1, /device:TPU:1, one launch (start us, length us, event | category | flops | bytes accessed | tf_op | source)
XLA Modules:
  0.0 430.3 jit_solution(6280213818727028009)
XLA Ops:
  8.1 2.1 copy.85
  10.2 0.8 copy.89
  11.1 0.2 reduce_window_sum.11
  11.4 0.1 select_reduce_fusion
  11.5 0.1 copy.94
  11.6 0.1 reshape.285
  11.7 1.7 gather_fusion
  13.4 8.4 %all-to-all-start.1 = ((bf16[16,4,2,16,256]{4,3,2,1,0:T(8,128)(2,1)}), bf16[16,4,2,16,256]{4,3,2,1,0:T(8,128)(2,1)S(1)}, u32[]{:S(2)}, u32[]{:S(2)}) async-start(bf16[16,4,2,16,256]{4,3,2,1,0:T(8,128)(2,1)} %bitcast.10), calls=%async_computation.2 | async-start | bytes 2097152 | tf_op jit(solution)/shard_map/all_to_all | solution.py:95
  21.8 1.2 copy.82
  23.1 19.3 %all-to-all-done.1 = bf16[16,4,2,16,256]{4,3,2,1,0:T(8,128)(2,1)S(1)} async-done(((bf16[16,4,2,16,256]{4,3,2,1,0:T(8,128)(2,1)}), bf16[16,4,2,16,256]{4,3,2,1,0:T(8,128)(2,1)S(1)}, u32[]{:S(2)}, u32[]{:S(2)}) %all-to-all-start.1) | async-done | bytes 1048608 | tf_op jit(solution)/shard_map/all_to_all | solution.py:95
  42.4 4.3 stack.2
  46.6 6.2 %all-to-all-start = ((bf16[16,1024,256]{1,2,0:T(8,128)(2,1)}), bf16[16,1024,256]{1,2,0:T(8,128)(2,1)}, u32[]{:S(2)}, u32[]{:S(2)}) async-start(bf16[16,1024,256]{1,2,0:T(8,128)(2,1)} %stack.2), calls=%async_computation | async-start | bytes 16777216 | tf_op jit(solution)/shard_map/all_to_all | solution.py:14
  52.9 0.1 copy.95
  53.0 0.2 copy.97
  53.2 0.1 copy.99
  53.4 0.2 convert_reduce_fusion
  53.6 1.2 fusion.20
  54.8 0.6 gather_fusion.1
  55.5 0.1 concatenate.21
  55.7 0.1 concatenate.24
  55.9 0.4 copy.100
  56.3 6.1 %fusion.65 = (f32[2,512]{1,0:T(2,128)S(1)}, bf16[2,512,1536]{1,2,0:T(8,128)(2,1)}) fusion(pred[512,1536]{0,1:T(8,128)(4,1)S(1)} %fusion.20, bf16[512,2,128]{2,0,1:T(8,128)(2,1)S(1)} %copy.97, bf16[1024,2,128]{2,0,1:T(8,128)(2,1)S(1)} %copy.96, bf16[512,256]{1,0:T(8,128)(2,1)} %param.17), kind=kOutput, calls=%fused_computation.93 | convolution fusion | flops 413664768 | bytes 4984832 | tf_op jit(solution)/shard_map/sub | solution.py:119
  62.4 2.5 fusion.28
  65.0 3.3 convolution_convert_fusion.1
  68.3 0.2 reduce-scatter.3.cloned.1.call-start
  68.6 0.7 add_reduce_fusion
  69.3 0.2 copy.84
  69.5 0.3 copy.87
  69.7 121.1 %all-to-all-done = bf16[16,1024,256]{1,2,0:T(8,128)(2,1)} async-done(((bf16[16,1024,256]{1,2,0:T(8,128)(2,1)}), bf16[16,1024,256]{1,2,0:T(8,128)(2,1)}, u32[]{:S(2)}, u32[]{:S(2)}) %all-to-all-start) | async-done | bytes 8388640 | tf_op jit(solution)/shard_map/all_to_all | solution.py:14
  190.8 12.3 %copy.83 = bf16[16,1024,256]{2,1,0:T(8,128)(2,1)} copy(bf16[16,1024,256]{1,2,0:T(8,128)(2,1)} %all-to-all-done) | data formatting | bytes 16777216 | tf_op jit(solution)/shard_map/all_to_all | solution.py:14
  203.1 12.0 %copy.86 = bf16[16384,256]{0,1:T(8,128)(2,1)} copy(bf16[16384,256]{1,0:T(8,128)(2,1)} %bitcast.76) | data formatting | bytes 16777216
  215.2 31.6 %while.18 = (s32[]{:T(128)}, f32[2,1024,128]{2,1,0:T(8,128)S(1)}, f32[2,1024]{1,0:T(2,128)S(1)}, f32[2,1024]{1,0:T(2,128)S(1)}, s32[]{:T(128)}, /*index=5*/bf16[...) while((s32[]{:T(128)}, f32[2,1024,128]{2,1,0:T(8,128)S(1)}, ...), condition=%wide.region_6.7_spmd.clone, body=%wide.region_1.6_spmd.clone.sunk | while | flops 1102583808 | bytes 35283264 | solution.py:71
  215.9 10.0 %conditional.3 = ((f32[2,1024,128]{2,1,0:T(8,128)S(1)}, f32[2,1024]{1,0:T(2,128)S(1)}, f32[2,1024]{1,0:T(2,128)S(1)})) conditional(s32[]{:T(128)} %convert_element_type.77, (f32[2,1024,128]{2,1,0:T(8,128)S(1)}, f32[2,1024]{1,0:T(2,128)S(1)}, f32[2,1024]{1,0:T(2,128)S(1)}) %tuple.68, (s32[]{:T(128)}, s32[]{:T(128)}, bf16[16384,256]{0,1:T(8,128)(2,1)}, ...), branch_computations={%region_2.0_spmd, %region_3.5_spmd} | conditional | flops 1102583808 | bytes 35278928 | solution.py:69
  215.9 1.3 constant_dynamic-slice_fusion
  217.2 0.7 broadcast_compare_fusion
  217.9 2.0 fusion.2
  219.9 2.3 fusion.3
  222.2 3.7 fusion.8
  226.6 10.0 %conditional.3 = ((f32[2,1024,128]{2,1,0:T(8,128)S(1)}, f32[2,1024]{1,0:T(2,128)S(1)}, f32[2,1024]{1,0:T(2,128)S(1)})) conditional(s32[]{:T(128)} %convert_element_type.77, (f32[2,1024,128]{2,1,0:T(8,128)S(1)}, f32[2,1024]{1,0:T(2,128)S(1)}, f32[2,1024]{1,0:T(2,128)S(1)}) %tuple.68, (s32[]{:T(128)}, s32[]{:T(128)}, bf16[16384,256]{0,1:T(8,128)(2,1)}, ...), branch_computations={%region_2.0_spmd, %region_3.5_spmd} | conditional | flops 1102583808 | bytes 35278928 | solution.py:69
  226.6 1.3 constant_dynamic-slice_fusion
  227.9 0.7 broadcast_compare_fusion
  228.6 2.0 fusion.2
  230.6 2.3 fusion.3
  232.9 3.7 fusion.8
  246.8 0.3 copy.88
  247.1 0.1 divide_convert_fusion
  247.2 4.5 %convolution_convert_fusion = bf16[1024,2048]{1,0:T(8,128)(2,1)} fusion(bf16[1024,256]{0,1:T(8,128)(2,1)S(1)} %bitcast.80, bf16[2048,2048]{1,0:T(8,128)(2,1)} %param.23, s32[]{:T(128)S(6)} %select_n.90), kind=kOutput, calls=%fused_computation.25 | convolution fusion | flops 1075838976 | bytes 5767172 | tf_op jit(solution)/shard_map/dot_general | solution.py:145
  251.8 171.1 %reduce-scatter.3.cloned.1.call-done = bf16[128,2048]{1,0:T(8,128)(2,1)} async-done(((bf16[1024,2048]{1,0:T(8,128)(2,1)}), bf16[128,2048]{1,0:T(8,128)(2,1)}) %reduce-scatter.3.cloned.1.call-update) | async-done | bytes 524304 | tf_op jit(solution)/shard_map/reduce_scatter | solution.py:144
  (75 shorter events, 0.9 us)
Async XLA Ops:
  8.0 3.7 copy-start
  8.0 207.1 %all-gather.2.cloned.1.call-start = ((), (), s32[]{:S(2)}) async-start(), calls=%async_computation.4 | async-start | bytes 8912896 | tf_op jit(solution)/shard_map/all_gather | solution.py:52
  13.4 29.0 %all-to-all-start.1 = ((bf16[16,4,2,16,256]{4,3,2,1,0:T(8,128)(2,1)}), bf16[16,4,2,16,256]{4,3,2,1,0:T(8,128)(2,1)S(1)}, u32[]{:S(2)}, u32[]{:S(2)}) async-start(bf16[16,4,2,16,256]{4,3,2,1,0:T(8,128)(2,1)} %bitcast.10), calls=%async_computation.2 | async-start | bytes 2097152 | tf_op jit(solution)/shard_map/all_to_all | solution.py:95
  46.6 6.2 %copy-start.3 = (bf16[512,256]{1,0:T(8,128)(2,1)S(1)}, bf16[512,256]{1,0:T(8,128)(2,1)}, u32[]{:S(2)}) copy-start(bf16[512,256]{1,0:T(8,128)(2,1)} %param.18) | copy-start | bytes 786436
  46.6 6.6 %copy-start.4 = (bf16[512,256]{1,0:T(8,128)(2,1)S(1)}, bf16[512,256]{1,0:T(8,128)(2,1)}, u32[]{:S(2)}) copy-start(bf16[512,256]{1,0:T(8,128)(2,1)} %param.19) | copy-start | bytes 786436
  46.6 7.0 %copy-start.6 = (s32[1,512]{1,0:T(1,128)S(1)}, s32[1,512]{1,0:T(1,128)}, u32[]{:S(2)}) copy-start(s32[1,512]{1,0:T(1,128)} %param.20) | copy-start | bytes 6148
  46.6 7.0 %copy-start.5 = (s32[1536]{0:T(1024)S(1)}, s32[1536]{0:T(1024)}, u32[]{:S(2)}) copy-start(s32[1536]{0:T(1024)} %constant.138.clone.1) | copy-start | bytes 18436
  46.6 144.2 %all-to-all-start = ((bf16[16,1024,256]{1,2,0:T(8,128)(2,1)}), bf16[16,1024,256]{1,2,0:T(8,128)(2,1)}, u32[]{:S(2)}, u32[]{:S(2)}) async-start(bf16[16,1024,256]{1,2,0:T(8,128)(2,1)} %stack.2), calls=%async_computation | async-start | bytes 16777216 | tf_op jit(solution)/shard_map/all_to_all | solution.py:14
  52.8 198.9 %reduce-scatter.5.cloned.1.call-start = ((), (), s32[]{:S(2)}) async-start(), calls=%async_computation.6 | async-start | bytes 2359296 | tf_op jit(solution)/shard_map/reduce_scatter | solution.py:150
  62.4 6.8 %copy-start.2 = (bf16[1024,256]{1,0:T(8,128)(2,1)S(1)}, bf16[1024,256]{1,0:T(8,128)(2,1)}, u32[]{:S(2)}) copy-start(bf16[1024,256]{1,0:T(8,128)(2,1)} %param.14) | copy-start | bytes 1572868
  68.3 354.5 %reduce-scatter.3.cloned.1.call-start = ((), (), s32[]{:S(2)}) async-start(), calls=%async_computation.5 | async-start | bytes 4718592 | tf_op jit(solution)/shard_map/reduce_scatter | solution.py:144
  246.8 176.1 %copy-start.1 = (bf16[64,2,16,256]{3,2,1,0:T(8,128)(2,1)S(1)}, bf16[64,2,16,256]{3,2,1,0:T(8,128)(2,1)}, u32[]{:S(2)}) copy-start(bf16[64,2,16,256]{3,2,1,0:T(8,128)(2,1)} %param.21) | copy-start | bytes 3145732
Sparse Core Ops, SparseCore 0:
  11.9 177.9 all-gather.1
Sparse Core Ops, SparseCore 1:
  68.4 119.3 reduce-scatter.4
  251.8 170.9 reduce-scatter.2
